TPU v7x, 256 devices: a whole 4x4x8 slice. The times are simulated.
256 devices in a mesh: obs: 4 (over y), blk: 64 (over x, z, core).
Axes of the slice: x: 4, y: 4, z: 8, core: 2. Of those that a mesh axis runs over, the one named last changes fastest.
Arguments:
- design_tiles: float32 [32768, 8, 128], P(('obs', 'blk')), may hold values from -8 to 8
- block_ids: int32 [32768, 8], P(('obs', 'blk')), may hold values from 0 to 63, as said below
- obs_weight: float32 [32768], P(('obs', 'blk')), may hold values from 4.8828126e-05 to 0.00048828125
- block_owner: int32 [64], replicated, may hold values from 0 to 63, each once
- prior_weight: float32 [512], replicated, may hold values from 0.25 to 1
Outputs:
- panel_factor: float32 [8192, 256], P('blk')
- panel_update: float32 [8192, 256], P('blk')
Inputs may be any that keep to these rules, and one draw needn't show every extreme that they name: `block_ids`: the 8 blocks of an observation are distinct. Among the 128 observations of one device (aligned blocks of rows) no block is named by more than 24 of them, and in every draw some device has a block named by exactly 24. `block_owner`: A permutation: each owner index once.
All inputs are finite; a program needn't handle non-finite values.
Results may differ from a plain program's by a relative error of at most 0.0003.
Values sent between devices are 32-bit elements; how exact they have to be, the bound alone decides.
No kernel may reach another device: no remote copies, remote signals or barrier semaphores. Data moves between devices by JAX's collectives and lax.ppermute only.
A program may use at most 64 MiB of HBM per device.

v0:
```python
import jax
import jax.numpy as jnp
from jax import lax
from jax.sharding import PartitionSpec as P


def back_solve(factor, right_rows):
    return jax.scipy.linalg.solve_triangular(factor, right_rows.T, lower=True).T


def with_prior(owned, row_index, prior_weight):
    col_index = jnp.arange(prior_weight.shape[0], dtype=jnp.int32)
    return owned + jnp.where(col_index[None, :] == row_index[:, None], prior_weight[None, :], 0.0)


def placed_square(owned, row_index, panel_cols):
    col_index = jnp.arange(panel_cols, dtype=jnp.int32)
    placing = (row_index[:, None] == col_index[None, :]).astype(jnp.float32)
    return jnp.einsum("rq,rp->qp", placing, owned, precision=lax.Precision.HIGHEST)


def finish_rows(owned, square, half_cols):
    mirrored = 0.5 * (square + square.T)
    factor = jnp.linalg.cholesky(mirrored[:half_cols, :half_cols])
    coupling = back_solve(factor, mirrored[half_cols:, :half_cols])
    first_rows = back_solve(factor, owned[:, :half_cols])
    update_rows = owned[:, half_cols:] - jnp.dot(
        first_rows, coupling.T, precision=lax.Precision.HIGHEST, preferred_element_type=jnp.float32
    )
    return (first_rows, update_rows)


def select_columns(labels, design_tiles, wanted):
    touched = design_tiles.shape[1]
    columns = jnp.zeros(
        (design_tiles.shape[0], wanted.shape[0], design_tiles.shape[2]), jnp.float32
    )
    for entry in range(touched):
        hit = labels[:, entry, None] == wanted[None, :]
        columns = columns + jnp.where(hit[:, :, None], design_tiles[:, entry, None, :], 0.0)
    return columns.reshape(design_tiles.shape[0], wanted.shape[0] * design_tiles.shape[2])


def local(design_tiles, block_ids, obs_weight, block_owner, prior_weight):
    block_width = design_tiles.shape[2]
    block_count = block_owner.shape[0]
    panel_cols = prior_weight.shape[0]
    half_cols = panel_cols // 2
    panel_blocks = panel_cols // block_width
    block_range = jnp.arange(block_count, dtype=jnp.int32)
    owner_index = lax.axis_index("blk")
    owner_block = jnp.sum(jnp.where(block_owner == owner_index, block_range, 0))
    slots = jnp.sum(
        jnp.where(
            block_ids[:, :, None] == block_range[None, None, :], block_owner[None, None, :], 0
        ),
        axis=2,
    )
    panel_design = select_columns(
        block_ids, design_tiles, jnp.arange(panel_blocks, dtype=jnp.int32)
    )
    weighted = panel_design * obs_weight[:, None]
    wanted = jnp.arange(lax.axis_size("blk") * block_width // block_width, dtype=jnp.int32)
    columns = select_columns(slots, design_tiles, wanted)
    partial_value = lax.psum_scatter(
        jnp.einsum("oi,op->ip", columns, weighted, precision=lax.Precision.HIGHEST),
        "blk",
        scatter_dimension=0,
        tiled=True,
    )
    owned = lax.psum(partial_value, "obs")
    row_index = owner_block * block_width + jnp.arange(block_width, dtype=jnp.int32)
    owned = with_prior(owned, row_index, prior_weight)
    square = lax.psum(placed_square(owned, row_index, panel_cols), "blk")
    first_rows, update_rows = finish_rows(owned, square, half_cols)
    return (first_rows, update_rows)


def solution(mesh):
    in_specs = (P(("obs", "blk"), None, None), P(("obs", "blk"), None), P(("obs", "blk")), P(), P())
    out_specs = (P("blk", None), P("blk", None))
    return jax.shard_map(local, mesh=mesh, in_specs=in_specs, out_specs=out_specs, check_vma=False)
```

profile of v0, /device:TPU:1, one launch (start us, length us, event | category | flops | bytes accessed | tf_op | source)
XLA Modules:
  0.0 546.3 jit_solution(13729939461648007592)
XLA Ops:
  7.2 0.0 reduce-scatter.2.cloned.1.call-start
  7.2 1.0 slice_bitcast_fusion.15
  8.2 0.8 select_reduce_fusion
  9.0 3.5 fusion.27
  12.5 0.1 iota_compare_fusion.14
  12.6 0.1 iota_compare_fusion.16
  12.8 0.1 iota_compare_fusion.18
  12.9 0.1 iota_compare_fusion.20
  13.0 0.1 iota_compare_fusion.6
  13.1 0.1 iota_compare_fusion.8
  13.2 0.1 iota_compare_fusion.10
  13.3 0.1 iota_compare_fusion.12
  13.4 9.0 %select_add_fusion = f32[128,64,128]{2,1,0:T(8,128)S(1)} fusion(f32[128,128]{1,0:T(8,128)S(1)} %bitcast.108, f32[128,128]{1,0:T(8,128)S(1)} %bitcast.110, f32[128,128]{1,0:T(8,128)S(1)} %bitcast.98, f32[128,128]{1,0:T(8,128)S(1)} %bitcast.100, f32[128,128]{1,0:T(8,128)S(1)} %bitcast.102, f32[128,128]{1,0:T(8,128)S(1)} %bitcast.104, ...), kind=kLoop, calls=%fused_computation.5 | loop fusion | flops 15728640 | bytes 4784128 | tf_op jit(solution)/shard_map/add | solution.py:40
  22.4 1.6 add_multiply_fusion
  23.9 18.2 %fusion = f32[8192,512]{1,0:T(8,128)} fusion(f32[16,8,64,128]{3,2,1,0:T(8,128)S(1)} %bitcast.94, f32[16,8,4,128]{3,2,1,0:T(4,128)S(1)} %bitcast.95), kind=kOutput, calls=%fused_computation.2 | convolution fusion | flops 6442450944 | bytes 21233664 | tf_op jit(solution)/shard_map/oi,op->ip/dot_general | solution.py:66
  42.2 0.0 all-reduce.4.cloned.1.call-start
  42.2 189.7 %reduce-scatter.2.cloned.1.call-done = f32[128,512]{1,0:T(8,128)} async-done(((f32[8192,512]{1,0:T(8,128)}), f32[128,512]{1,0:T(8,128)}) %reduce-scatter.2.cloned.1.call-update) | async-done | bytes 262160 | tf_op jit(solution)/shard_map/reduce_scatter | solution.py:65
  231.9 0.2 all-reduce.6.cloned.1.call-start
  232.2 0.6 fusion.24
  233.4 48.2 %all-reduce.4.cloned.1.call-done = f32[128,512]{1,0:T(8,128)} async-done(((f32[128,512]{1,0:T(8,128)}), f32[128,512]{1,0:T(8,128)}) %all-reduce.4.cloned.1.call-update) | async-done | bytes 262160 | tf_op jit(solution)/shard_map/psum | solution.py:71
  281.6 1.0 select_add_fusion.1
  282.7 1.7 fusion.10
  284.4 188.1 %all-reduce.6.cloned.1.call-done = f32[512,512]{1,0:T(8,128)} async-done(((f32[512,512]{1,0:T(8,128)}), f32[512,512]{1,0:T(8,128)}) %all-reduce.6.cloned.1.call-update) | async-done | bytes 1048592 | tf_op jit(solution)/shard_map/psum | solution.py:74
  472.6 1.6 copy.11
  474.1 1.4 fusion.3
  475.6 0.1 copy.12
  475.8 11.7 %cholesky.50 = f32[128,128]{1,0:T(8,128)S(1)} custom-call(f32[128,128]{1,0:T(8,128)S(1)} %cholesky.118), custom_call_target="Cholesky" | custom-call | tf_op jit(solution)/shard_map/jit(cholesky)/cholesky | solution.py:24
  487.6 9.8 %custom-call.18 = f32[1,128,128]{1,2,0:T(8,128)S(1)} custom-call(f32[1,128,128]{2,1,0:T(8,128)S(1)} %get-tuple-element.37), custom_call_target="InvertDiagBlocksLowerTriangular" | custom-call | tf_op jit(solution)/shard_map/jit(cholesky)/cholesky | solution.py:24
  497.4 0.2 constant_dynamic-update-slice_fusion.1
  497.6 0.3 convolution_subtract_fusion.3
  497.9 11.7 %cholesky.105 = f32[128,128]{1,0:T(8,128)S(1)} custom-call(f32[128,128]{1,0:T(8,128)S(1)} %convolution_subtract_fusion.3), custom_call_target="Cholesky" | custom-call | tf_op jit(solution)/shard_map/jit(cholesky)/cholesky | solution.py:24
  509.6 0.7 compare_reduce_fusion
  510.3 0.6 compare_reduce_fusion.1
  512.3 0.1 triangular_solve.72
  512.4 4.1 while.1
  512.6 0.6 fusion.36
  513.1 1.4 bitcast_dynamic-update-slice_fusion.2
  514.5 0.6 fusion.36
  515.1 1.4 bitcast_dynamic-update-slice_fusion.2
  516.5 19.7 %custom-call.19 = f32[2,128,128]{1,2,0:T(8,128)S(1)} custom-call(f32[2,128,128]{2,1,0:T(8,128)S(1)} %get-tuple-element.9), custom_call_target="InvertDiagBlocksLowerTriangular" | custom-call | tf_op jit(solution)/shard_map/jit(_solve_triangular)/triangular_solve | solution.py:8
  536.2 0.3 fusion.11
  536.5 0.3 convolution_subtract_fusion.1
  536.8 0.3 fusion.20
  537.1 0.3 fusion.15
  537.4 0.3 convolution_subtract_fusion.2
  537.7 0.3 fusion.21
  538.0 1.1 convolution_subtract_fusion
  539.1 0.8 copy.13
  (24 shorter events, 0.3 us)
Async XLA Ops:
  7.2 15.2 %copy-start.1 = (f32[128]{0:T(128)S(1)}, f32[128]{0:T(128)}, u32[]{:S(2)}) copy-start(f32[128]{0:T(128)} %param.7) | copy-start | bytes 1540
  7.2 224.7 %reduce-scatter.2.cloned.1.call-start = ((), (), s32[]{:S(2)}) async-start(), calls=%async_computation.1 | async-start | bytes 17039360 | tf_op jit(solution)/shard_map/reduce_scatter | solution.py:65
  42.1 190.0 %copy-start.2 = (s32[64]{0:T(128)S(1)}, s32[64]{0:T(128)}, u32[]{:S(2)}) copy-start(s32[64]{0:T(128)} %param.8) | copy-start | bytes 772
  42.1 239.5 %copy-start = (f32[512]{0:T(512)S(1)}, f32[512]{0:T(512)}, u32[]{:S(2)}) copy-start(f32[512]{0:T(512)} %param.9) | copy-start | bytes 6148
  42.2 239.5 %all-reduce.4.cloned.1.call-start = ((), (), s32[]{:S(2)}) async-start(), calls=%async_computation.2 | async-start | bytes 524288 | tf_op jit(solution)/shard_map/psum | solution.py:71
  231.9 240.7 %all-reduce.6.cloned.1.call-start = ((), (), s32[]{:S(2)}) async-start(), calls=%async_computation.3 | async-start | bytes 2097152 | tf_op jit(solution)/shard_map/psum | solution.py:74
Sparse Core Ops, SparseCore 0:
  42.3 189.5 reduce-scatter.1
  234.2 47.3 all-reduce.3
  285.0 187.4 all-reduce.5
where the time goes:
time: 548 us; the launch traced here: 546 us
  waiting for transfers between devices  426 us (78%)
  other arithmetic  69.7 us (13%)
  matrix products  23.1 us (4%)
  between operations  16 us (3%)
  local copies, waits for them, and re-layouts  11 us (2%)
    reduce_scatter x1, waiting for transfers between devices, local(): lax.psum_scatter(jnp.einsum('oi,op->ip', columns, weighted, precision=lax...  190 us
    psum x1, waiting for transfers between devices, local(): square = lax.psum(placed_square(owned, row_index, panel_cols), 'blk')  188 us
    psum x1, waiting for transfers between devices, local(): owned = lax.psum(partial_value, 'obs')  48.2 us
    another operation x7, other arithmetic, finish_rows(): factor = jnp.linalg.cholesky(mirrored[:half_cols, :half_cols])  34.6 us
    another operation x3, other arithmetic, back_solve(): return jax.scipy.linalg.solve_triangular(factor, right_rows.T, lower=True).T  19.7 us
    dot_general x1, matrix products, local(): jnp.einsum('oi,op->ip', columns, weighted, precision=lax.Precision.HIGHEST)  18.2 us
  transfers between devices with their start and end apart: 3, of which 3 were waited for; matrix products, arithmetic and copies ran while one was open for 0% of the time, Pallas kernels for 0%

commit v1 on v0

v1 whole, which is shorter than its diff:
```python
import jax
import jax.numpy as jnp
from jax import lax
from jax.sharding import PartitionSpec as P

CAP = 24
HI = lax.Precision.HIGHEST


def back_solve(factor, right_rows):
    return jax.scipy.linalg.solve_triangular(factor, right_rows.T, lower=True).T


def select_columns(labels, design_tiles, wanted):
    touched = design_tiles.shape[1]
    columns = jnp.zeros(
        (design_tiles.shape[0], wanted.shape[0], design_tiles.shape[2]), jnp.float32
    )
    for entry in range(touched):
        hit = labels[:, entry, None] == wanted[None, :]
        columns = columns + jnp.where(hit[:, :, None], design_tiles[:, entry, None, :], 0.0)
    return columns.reshape(design_tiles.shape[0], wanted.shape[0] * design_tiles.shape[2])


def obs_butterfly(x):
    n = lax.axis_size("obs")
    step = 1
    while step < n:
        perm = [(i, i ^ step) for i in range(n)]
        x = x + lax.ppermute(x, "obs", perm)
        step *= 2
    return x


def local(design_tiles, block_ids, obs_weight, block_owner, prior_weight):
    n_obs, touched, bw = design_tiles.shape
    nblk = block_owner.shape[0]
    panel_cols = prior_weight.shape[0]
    half = panel_cols // 2
    panel_blocks = panel_cols // bw
    nb = lax.axis_size("blk")
    my_j = lax.axis_index("blk")
    block_range = jnp.arange(nblk, dtype=jnp.int32)
    dest_range = jnp.arange(nb, dtype=jnp.int32)

    inv_owner = jnp.sum(
        jnp.where(block_owner[None, :] == dest_range[:, None], block_range[None, :], 0), axis=1
    )
    slot_owner = jnp.sum(
        jnp.where(block_ids[:, :, None] == block_range[None, None, :], block_owner[None, None, :], 0),
        axis=2,
    )
    hit = slot_owner[:, :, None] == dest_range[None, None, :]
    touch = jnp.sum(hit.astype(jnp.int32), axis=1)
    cum = jnp.cumsum(touch, axis=0)
    rank_range = jnp.arange(CAP, dtype=jnp.int32)
    obs_sel = jnp.sum((cum[:, :, None] <= rank_range[None, None, :]).astype(jnp.int32), axis=0)
    valid = rank_range[None, :] < cum[-1][:, None]
    obs_sel = jnp.minimum(obs_sel, n_obs - 1)
    owners_sel = slot_owner[obs_sel]
    k_sel = jnp.sum(
        jnp.where(owners_sel == dest_range[:, None, None], jnp.arange(touched, dtype=jnp.int32), 0),
        axis=2,
    )
    flat_tiles = design_tiles.reshape(n_obs * touched, bw)
    tile_rows = flat_tiles[obs_sel * touched + k_sel]

    panel_design = select_columns(
        block_ids, design_tiles, jnp.arange(panel_blocks, dtype=jnp.int32)
    )
    weighted = panel_design * obs_weight[:, None]
    panel_rows = weighted[obs_sel]
    tile_rows = jnp.where(valid[:, :, None], tile_rows, 0.0)
    panel_rows = jnp.where(valid[:, :, None], panel_rows, 0.0)

    gram = jnp.einsum("op,oq->pq", weighted, panel_design[:, :half], precision=HI)
    gram_rows = panel_cols // nb
    payload = jnp.concatenate(
        [
            tile_rows.reshape(nb, CAP * bw),
            panel_rows.reshape(nb, CAP * panel_cols),
            gram.reshape(nb, gram_rows * half),
        ],
        axis=1,
    )
    got = lax.all_to_all(payload, "blk", 0, 0, tiled=True)
    got_tiles = got[:, : CAP * bw].reshape(nb * CAP, bw)
    got_panel = got[:, CAP * bw : CAP * (bw + panel_cols)].reshape(nb * CAP, panel_cols)
    got_gram = got[:, CAP * (bw + panel_cols) :].reshape(nb, gram_rows * half)
    owned = jnp.einsum("si,sp->ip", got_tiles, got_panel, precision=HI)
    gram_part = jnp.sum(got_gram, axis=0)

    both = obs_butterfly(jnp.concatenate([owned.reshape(-1), gram_part]))
    owned = both[: bw * panel_cols].reshape(bw, panel_cols)
    gram_part = both[bw * panel_cols :]

    spread = jnp.broadcast_to(gram_part[None, :], (nb, gram_rows * half))
    square = lax.all_to_all(spread, "blk", 0, 0, tiled=True).reshape(panel_cols, half)
    diag = jnp.arange(half, dtype=jnp.int32)
    square = square.at[diag, diag].add(prior_weight[:half])

    my_block = jnp.sum(jnp.where(block_owner == my_j, block_range, 0))
    row_index = my_block * bw + jnp.arange(bw, dtype=jnp.int32)
    col_index = jnp.arange(panel_cols, dtype=jnp.int32)
    owned = owned + jnp.where(col_index[None, :] == row_index[:, None], prior_weight[None, :], 0.0)

    top = square[:half]
    mirrored = 0.5 * (top + top.T)
    factor = jnp.linalg.cholesky(mirrored)
    coupling = back_solve(factor, square[half:])
    first_rows = back_solve(factor, owned[:, :half])
    update_rows = owned[:, half:] - jnp.dot(
        first_rows, coupling.T, precision=HI, preferred_element_type=jnp.float32
    )
    return (first_rows, update_rows)


def solution(mesh):
    in_specs = (P(("obs", "blk"), None, None), P(("obs", "blk"), None), P(("obs", "blk")), P(), P())
    out_specs = (P("blk", None), P("blk", None))
    return jax.shard_map(local, mesh=mesh, in_specs=in_specs, out_specs=out_specs, check_vma=False)
```

time: 548 us -> 279 us (0.51)
  waiting for transfers between devices: 426 us -> 27.1 us
  blocking collectives: 0 us -> 115 us
  local copies, waits for them, and re-layouts: 11 us -> 36.5 us
  matrix products: 23.1 us -> 7.46 us
  between operations: 16 us -> 3.21 us
  starting transfers between devices: 0.3 us -> 12.1 us
  other arithmetic: 69.7 us -> 77.2 us
    psum x2 -> x0, waiting for transfers between devices: 236 us -> none  [the longest x1 188 us: local(): square = lax.psum(placed_square(owned, row_index, panel_cols), 'blk')]
    reduce_scatter x1 -> x0, waiting for transfers between devices: 190 us -> none  [local(): lax.psum_scatter(jnp.einsum('oi,op->ip', columns, weighted, precision=lax...]
    all_to_all x0 -> x1, blocking collectives: none -> 115 us  [local(): got = lax.all_to_all(payload, 'blk', 0, 0, tiled=True)]
    dot_general x3, matrix products: 20.9 us -> 5.33 us  [the longest x1 4.12 us: local(): owned = jnp.einsum('si,sp->ip', got_tiles, got_panel, precision=HI)]
    all_to_all x0 -> x1, waiting for transfers between devices: none -> 15.6 us  [local(): lax.all_to_all(spread, 'blk', 0, 0, tiled=True).reshape(panel_cols, half)]
    scatter-add x0 -> x1, other arithmetic: none -> 13.4 us  [local(): square = square.at[diag, diag].add(prior_weight[:half])]
    ppermute x0 -> x2, waiting for transfers between devices: none -> 11.5 us  [obs_butterfly(): x = x + lax.ppermute(x, 'obs', perm)]
    gather x0 -> x3, local copies, waits for them, and re-layouts: none -> 8.95 us  [the longest x1 3.76 us: local(): panel_rows = weighted[obs_sel]]
where the time goes in v1:
time: 279 us; the launch traced here: 278 us
  blocking collectives  115 us (41%)
  other arithmetic  77.2 us (28%)
  local copies, waits for them, and re-layouts  36.5 us (13%)
  waiting for transfers between devices  27.1 us (10%)
  starting transfers between devices  12.1 us (4%)
  matrix products  7.46 us (3%)
  between operations  3.21 us (1%)
    all_to_all x1, blocking collectives, local(): got = lax.all_to_all(payload, 'blk', 0, 0, tiled=True)  115 us
    another operation x7, other arithmetic, local(): factor = jnp.linalg.cholesky(mirrored)  34.7 us
    another operation x3, other arithmetic, back_solve(): return jax.scipy.linalg.solve_triangular(factor, right_rows.T, lower=True).T  20 us
    all_to_all x1, waiting for transfers between devices, local(): lax.all_to_all(spread, 'blk', 0, 0, tiled=True).reshape(panel_cols, half)  15.6 us
    scatter-add x1, other arithmetic, local(): square = square.at[diag, diag].add(prior_weight[:half])  13.4 us
    ppermute x2, waiting for transfers between devices, obs_butterfly(): x = x + lax.ppermute(x, 'obs', perm)  11.5 us
    all_to_all x1, starting transfers between devices, local(): lax.all_to_all(spread, 'blk', 0, 0, tiled=True).reshape(panel_cols, half)  7.76 us
    unnamed x19, local copies, waits for them, and re-layouts  7.71 us
  transfers between devices with their start and end apart: 3, of which 3 were waited for; matrix products, arithmetic and copies ran while one was open for 0% of the time, Pallas kernels for 0%

profile of v1, /device:TPU:1, one launch (start us, length us, event | category | flops | bytes accessed | tf_op | source)
XLA Modules:
  0.0 278.3 jit_solution(5970961260448407696)
XLA Ops:
  0.6 1.0 slice_bitcast_fusion.15
  1.6 0.8 select_reduce_fusion.1
  2.9 3.5 %fusion.27 = (f32[128,1,128]{2,1,0:T(1,128)S(1)}, f32[128,1,128]{2,1,0:T(1,128)S(1)}, f32[128,1,128]{2,1,0:T(1,128)S(1)}, f32[128,1,128]{2,1,0:T(1,128)S(1)}, f3...) fusion(f32[128,8,128]{2,1,0:T(8,128)} %param.5), kind=kLoop, calls=%fused_computation.105 | loop fusion | bytes 1048576 | tf_op jit(solution)/shard_map/slice | solution.py:21
  6.9 1.4 add_add_fusion
  8.3 0.7 broadcast_multiply_fusion
  9.0 0.6 fusion.7
  9.7 0.9 reshape.363
  10.5 1.2 convert_reduce_fusion
  11.8 3.8 %gather_fusion.2 = f32[1536,512]{1,0:T(8,128)S(1)} fusion(f32[128,512]{1,0:T(8,128)S(1)} %broadcast_multiply_fusion, s32[2048]{0:T(1024)S(1)} %pad_clamp_fusion.1), kind=kCustom, calls=%fused_computation.2 | custom fusion | bytes 6297600 | tf_op jit(solution)/shard_map/gather | solution.py:72
  15.7 0.3 broadcast_select_fusion
  16.0 3.5 %copy.51 = f32[8,8,24,512]{3,1,2,0:T(8,128)} copy(f32[8,8,24,512]{3,2,1,0:T(8,128)S(1)} %bitcast.115) | data formatting | bytes 6291456
  19.4 2.6 gather_fusion
  22.0 1.2 select_reduce_fusion
  23.3 2.6 gather_fusion.1
  26.4 1.4 copy-done.1
  28.1 3.2 %all_to_all.12 = f32[64,1,17408]{2,1,0:T(1,128)S(1)} reshape(f32[64,17408]{1,0:T(8,128)S(1)} %pad_maximum_fusion) | data formatting | bytes 8912896 | tf_op jit(solution)/shard_map/all_to_all | solution.py:86
  31.3 114.6 %all_to_all.18 = f32[64,1,17408]{2,1,0:T(1,128)S(1)} all-to-all(f32[64,1,17408]{2,1,0:T(1,128)S(1)} %all_to_all.12), channel_id=1, replica_groups=mesh['obs'=4,'blk'=64] {'blk'}, dimensions={0} | all-to-all | bytes 8912896 | tf_op jit(solution)/shard_map/all_to_all | solution.py:86
  146.0 0.8 copy.58
  146.8 0.9 slice.230
  147.9 2.1 reshape.364
  150.1 2.0 reshape.365
  152.0 4.1 %convolution_bitcast_fusion = f32[16,4,8,128]{3,2,1,0:T(8,128)S(1)} fusion(f32[1536,128]{1,0:T(8,128)} %reshape.364, f32[1536,512]{1,0:T(8,128)} %reshape.365), kind=kOutput, calls=%fused_computation.9 | convolution fusion | flops 1207959552 | bytes 4194304 | tf_op jit(solution)/shard_map/si,sp->ip/dot_general | solution.py:90
  156.3 1.4 collective-permute-start
  157.7 6.3 %collective-permute-done = f32[67584]{0:T(1024)S(1)} collective-permute-done((f32[67584]{0:T(1024)S(1)}, f32[67584]{0:T(1024)S(1)}, u32[]{:S(2)}, u32[]{:S(2)}) %collective-permute-start) | collective-permute-done | bytes 270368 | tf_op jit(solution)/shard_map/ppermute | solution.py:30
  164.0 3.0 %collective-permute-start.1 = (f32[67584]{0:T(1024)S(1)}, f32[67584]{0:T(1024)S(1)}, u32[]{:S(2)}, u32[]{:S(2)}) collective-permute-start(f32[67584]{0:T(1024)S(1)} %fusion.24), channel_id=1, source_target_pairs={{0,128},{64,192},{128,0},{192,64},{1,129},{65,193},{129,1},{193,65... | collective-permute-start | bytes 811016 | tf_op jit(solution)/shard_map/ppermute | solution.py:30
  167.0 5.3 %collective-permute-done.1 = f32[67584]{0:T(1024)S(1)} collective-permute-done((f32[67584]{0:T(1024)S(1)}, f32[67584]{0:T(1024)S(1)}, u32[]{:S(2)}, u32[]{:S(2)}) %collective-permute-start.1) | collective-permute-done | bytes 270368 | tf_op jit(solution)/shard_map/ppermute | solution.py:30
  172.3 1.1 broadcast_in_dim.250
  173.4 7.8 %all-to-all-start.1 = ((f32[64,1,2048]{2,1,0:T(1,128)}), f32[64,1,2048]{2,1,0:T(1,128)S(1)}, u32[]{:S(2)}, u32[]{:S(2)}) async-start(f32[64,1,2048]{2,1,0:T(1,128)} %broadcast_in_dim.250), calls=%async_computation.1 | async-start | bytes 1048576 | tf_op jit(solution)/shard_map/all_to_all | solution.py:98
  181.2 0.6 fusion.22
  182.9 15.6 %all-to-all-done.1 = f32[64,1,2048]{2,1,0:T(1,128)S(1)} async-done(((f32[64,1,2048]{2,1,0:T(1,128)}), f32[64,1,2048]{2,1,0:T(1,128)S(1)}, u32[]{:S(2)}, u32[]{:S(2)}) %all-to-all-start.1) | async-done | bytes 524320 | tf_op jit(solution)/shard_map/all_to_all | solution.py:98
  198.4 1.3 reduce.12
  199.8 13.4 %scatter_fusion = f32[512,256]{1,0:T(8,128)S(1)} fusion(f32[512,256]{1,0:T(8,128)S(1)} %reshape.367, s32[256]{0:T(256)S(1)} %bitcast.113, f32[256]{0:T(256)S(1)} %slice-done), kind=kCustom, calls=%fused_computation.3 | custom fusion | flops 256 | bytes 5120 | tf_op jit(solution)/shard_map/scatter-add | solution.py:100
  213.7 11.7 %cholesky.50 = f32[128,128]{1,0:T(8,128)S(1)} custom-call(f32[128,128]{1,0:T(8,128)S(1)} %cholesky.118), custom_call_target="Cholesky" | custom-call | tf_op jit(solution)/shard_map/jit(cholesky)/cholesky | solution.py:109
  225.4 9.8 %custom-call.18 = f32[1,128,128]{1,2,0:T(8,128)S(1)} custom-call(f32[1,128,128]{2,1,0:T(8,128)S(1)} %get-tuple-element.43), custom_call_target="InvertDiagBlocksLowerTriangular" | custom-call | tf_op jit(solution)/shard_map/jit(cholesky)/cholesky | solution.py:109
  235.7 11.7 %cholesky.105 = f32[128,128]{1,0:T(8,128)S(1)} custom-call(f32[128,128]{1,0:T(8,128)S(1)} %convolution_subtract_fusion.3), custom_call_target="Cholesky" | custom-call | tf_op jit(solution)/shard_map/jit(cholesky)/cholesky | solution.py:109
  247.5 0.6 compare_reduce_fusion.1
  248.1 0.7 compare_reduce_fusion
  250.3 4.1 %while.1 = (s32[]{:T(128)}, f32[256,256]{1,0:T(8,128)S(1)}, s32[2,2]{1,0:T(2,128)S(1)}, f32[2,128,128]{2,1,0:T(8,128)S(1)}, s32[]{:T(128)}) while((s32[]{:T(128)}, f32[256,256]{1,0:T(8,128)S(1)}, s32[2,2]{1,0:T(2,128)S(1)}, f32[2,128,128]{2,1,0:T(8,128)S(1)}, s32[]{:T(128)}) %tuple.50), condition=%wide.while_cond, body=%wide.while_body.sunk | while | flops 2 | bytes 131189 | solution.py:11
  250.3 0.6 fusion.38
  250.9 1.4 bitcast_dynamic-update-slice_fusion.2
  252.4 0.6 fusion.38
  253.0 1.4 bitcast_dynamic-update-slice_fusion.2
  254.4 19.9 %custom-call.19 = f32[2,128,128]{1,2,0:T(8,128)S(1)} custom-call(f32[2,128,128]{2,1,0:T(8,128)S(1)} %get-tuple-element.9), custom_call_target="InvertDiagBlocksLowerTriangular" | custom-call | tf_op jit(solution)/shard_map/jit(_solve_triangular)/triangular_solve | solution.py:11
  275.2 0.8 copy.43
  276.0 0.3 fusion.5
  276.6 0.3 fusion.15
  276.9 0.6 convolution_subtract_fusion
  277.5 0.8 copy.44
  (70 shorter events, 5.0 us)
Async XLA Ops:
  19.4 3.9 %copy-start = (f32[128,8,128]{2,1,0:T(8,128)S(1)}, f32[128,8,128]{2,1,0:T(8,128)}, u32[]{:S(2)}) copy-start(f32[128,8,128]{2,1,0:T(8,128)} %param.5) | copy-start | bytes 1572868
  23.3 3.1 %copy-start.2 = (f32[64,2048]{1,0:T(8,128)S(1)}, f32[64,2048]{1,0:T(8,128)}, u32[]{:S(2)}) copy-start(f32[64,2048]{1,0:T(8,128)} %reshape.363) | copy-start | bytes 1572868
  25.9 1.9 copy-start.1
  156.2 25.0 %copy-start.4 = (s32[64]{0:T(128)S(1)}, s32[64]{0:T(128)}, u32[]{:S(2)}) copy-start(s32[64]{0:T(128)} %param.8) | copy-start | bytes 772
  156.2 26.5 %copy-start.3 = (f32[512]{0:T(512)S(1)}, f32[512]{0:T(512)}, u32[]{:S(2)}) copy-start(f32[512]{0:T(512)} %param.9) | copy-start | bytes 6148
  156.3 7.6 %collective-permute-start = (f32[67584]{0:T(1024)S(1)}, f32[67584]{0:T(1024)S(1)}, u32[]{:S(2)}, u32[]{:S(2)}) collective-permute-start(f32[67584]{0:T(1024)S(1)} %pad_maximum_fusion.1), channel_id=1, source_target_pairs={{0,64},{64,0},{128,192},{192,128},{1,65},{65,1},{129,193},{193,129... | collective-permute-start | bytes 811016 | tf_op jit(solution)/shard_map/ppermute | solution.py:30
  164.0 8.3 %collective-permute-start.1 = (f32[67584]{0:T(1024)S(1)}, f32[67584]{0:T(1024)S(1)}, u32[]{:S(2)}, u32[]{:S(2)}) collective-permute-start(f32[67584]{0:T(1024)S(1)} %fusion.24), channel_id=1, source_target_pairs={{0,128},{64,192},{128,0},{192,64},{1,129},{65,193},{129,1},{193,65... | collective-permute-start | bytes 811016 | tf_op jit(solution)/shard_map/ppermute | solution.py:30
  172.3 27.5 %slice-start = ((f32[512]{0:T(512)}), f32[256]{0:T(256)S(1)}, s32[]{:S(2)}) async-start(f32[512]{0:T(512)} %param.9), calls=%async_computation.2 | async-start | bytes 2048 | tf_op jit(solution)/shard_map/slice | solution.py:100
  173.4 25.1 %all-to-all-start.1 = ((f32[64,1,2048]{2,1,0:T(1,128)}), f32[64,1,2048]{2,1,0:T(1,128)S(1)}, u32[]{:S(2)}, u32[]{:S(2)}) async-start(f32[64,1,2048]{2,1,0:T(1,128)} %broadcast_in_dim.250), calls=%async_computation.1 | async-start | bytes 1048576 | tf_op jit(solution)/shard_map/all_to_all | solution.py:98
